TPU v7x, 32 devices: a whole 2x2x4 slice. The times are simulated.
32 devices in a mesh: gx: 8 (over z, y), gy: 4 (over x, core).
Axes of the slice: x: 2, y: 2, z: 4, core: 2. Of those that a mesh axis runs over, the one named last changes fastest.
Arguments:
- records: bfloat16 [128, 8, 8192], P('gx', 'gy')
- kept_bins: int32 [1024], replicated, may hold values from 1 to 4095, as said below
- pair_offsets: int32 [128], replicated, may hold values from 1 to 128, as said below
Outputs:
- correlation: bfloat16 [128, 128, 512], P('gy', 'gx')
Inputs may be any that keep to these rules, and one draw needn't show every extreme that they name: `kept_bins`: 1024 different bin indices in increasing order, both 1 and 4095 among them. `pair_offsets`: each offset from 1 to 128 exactly once, in any order.
All inputs are finite; a program needn't handle non-finite values.
Results may differ from a plain program's by a relative error of at most 0.0075.
Values may be sent and summed in bfloat16 or wider, within the bound.
No kernel may reach another device: no remote copies, remote signals or barrier semaphores. Data moves between devices by JAX's collectives and lax.ppermute only.
A program may use at most 64 MiB of HBM per device.

v0:
```python
import math
import jax
import jax.numpy as jnp
from jax import lax
from jax.sharding import PartitionSpec as P

SAMPLES = 8192
LAGS = 512


def inverse_table(kept_bins):
    lag_index = jnp.arange(LAGS, dtype=jnp.int32) - LAGS // 2
    angles = jnp.mod(kept_bins[:, None] * lag_index[None, :], SAMPLES).astype(jnp.float32) * (
        2.0 * math.pi / SAMPLES
    )
    return jnp.stack([jnp.cos(angles), -jnp.sin(angles)], axis=0).astype(jnp.bfloat16)


def whiten(spectra):
    mean_power = jnp.mean(spectra * spectra, axis=-1, keepdims=True)
    return (spectra * lax.rsqrt(mean_power + 1e-06)).astype(jnp.bfloat16)


def add_cross(running, window_block, my_offsets, own_count):
    group_size = math.gcd(8, my_offsets.shape[0])
    own_part = window_block[:, :own_count].astype(jnp.float32)

    def one_offset(shift_by):
        theirs = lax.dynamic_slice_in_dim(window_block, shift_by, own_count, 1).astype(jnp.float32)
        real_part = jnp.sum(
            own_part[:, :, 0] * theirs[:, :, 0] + own_part[:, :, 1] * theirs[:, :, 1], axis=0
        )
        imag_part = jnp.sum(
            own_part[:, :, 1] * theirs[:, :, 0] - own_part[:, :, 0] * theirs[:, :, 1], axis=0
        )
        return jnp.stack([real_part, imag_part], axis=1)

    def one_group(group_index, carried):
        chosen = lax.dynamic_slice_in_dim(my_offsets, group_index * group_size, group_size)
        update = jax.vmap(one_offset)(chosen)
        current = lax.dynamic_slice_in_dim(carried, group_index * group_size, group_size, 0)
        return lax.dynamic_update_slice_in_dim(
            carried, current + update, group_index * group_size, 0
        )

    return lax.fori_loop(0, my_offsets.shape[0] // group_size, one_group, running)


def small_table(kept_bins, rows):
    fine_count = 1 << (rows.bit_length() - 1) // 2
    coarse_count = rows // fine_count

    def angles(step, count):
        index = step * jnp.arange(count, dtype=jnp.int32)
        return jnp.mod(index[:, None] * kept_bins[None, :], SAMPLES).astype(jnp.float32) * (
            2.0 * math.pi / SAMPLES
        )

    fine = angles(1, fine_count)[None, :, :]
    coarse = angles(fine_count, coarse_count)[:, None, :]
    cos_f, sin_f, cos_c, sin_c = (jnp.cos(fine), jnp.sin(fine), jnp.cos(coarse), jnp.sin(coarse))
    cos_t = cos_f * cos_c - sin_f * sin_c
    sin_t = sin_f * cos_c + cos_f * sin_c
    table = jnp.concatenate([cos_t, -sin_t], axis=-1)
    return table.reshape(rows, 2 * kept_bins.shape[0]).astype(jnp.bfloat16)


def forward_spectra(record_rows, kept_bins):
    row_count, samples = record_rows.shape
    bin_count = kept_bins.shape[0]
    block_len = math.gcd(samples, 1024)
    block_count = samples // block_len
    x = record_rows.reshape(row_count, block_count, block_len).astype(jnp.float32)
    br = jnp.mod(
        jnp.arange(block_count, dtype=jnp.int32)[:, None]
        * jnp.arange(block_count, dtype=jnp.int32)[None, :],
        block_count,
    ).astype(jnp.float32) * (2.0 * math.pi / block_count)
    twiddle = jnp.stack([jnp.cos(br), -jnp.sin(br)], axis=0)
    y = jnp.einsum("ubs,pbr->prus", x, twiddle, precision=lax.Precision.HIGHEST)
    y_hi = y.astype(jnp.bfloat16)
    y_lo = (y - y_hi.astype(jnp.float32)).astype(jnp.bfloat16)
    lhs = jnp.stack([y_hi, y_lo], axis=0).reshape(-1, block_len)
    prod = jnp.dot(lhs, small_table(kept_bins, block_len), preferred_element_type=jnp.float32)
    prod = prod.reshape(2, 2, block_count, row_count, 2, bin_count)
    prod = prod[0] + prod[1]
    pick = (
        jnp.mod(kept_bins, block_count)[None, None, :]
        == jnp.arange(block_count, dtype=jnp.int32)[:, None, None]
    ).astype(jnp.float32)
    real_part = jnp.sum(pick * (prod[0, :, :, 0] - prod[1, :, :, 1]), axis=0)
    imag_part = jnp.sum(pick * (prod[0, :, :, 1] + prod[1, :, :, 0]), axis=0)
    return jnp.concatenate([real_part, imag_part], axis=-1)


def local(records, kept_bins, pair_offsets):
    ch_dev, win_dev, samples = records.shape
    bin_count = kept_bins.shape[0]
    band_span = pair_offsets.shape[0]
    record_rows = jnp.transpose(records, (1, 0, 2)).reshape(win_dev * ch_dev, samples)
    spectra = forward_spectra(record_rows, kept_bins)
    white = whiten(spectra).reshape(win_dev, ch_dev, 2, bin_count)
    off_dev = band_span // lax.axis_size("gy")
    my_offsets = lax.dynamic_slice_in_dim(pair_offsets, lax.axis_index("gy") * off_dev, off_dev)
    inverse = inverse_table(kept_bins)
    norm_scale = 0.5 / math.sqrt(win_dev * lax.axis_size("gy") * bin_count)
    freq_white = lax.all_to_all(white, "gx", split_axis=3, concat_axis=1, tiled=True)
    all_channels = freq_white.shape[1]
    empty_sum = jnp.zeros((off_dev, all_channels, 2, freq_white.shape[3]), jnp.float32)
    window_block = lax.all_gather(freq_white, "gy", axis=0, tiled=True)
    widened = jnp.concatenate(
        [
            window_block,
            jnp.zeros(
                (window_block.shape[0], band_span, 2, window_block.shape[3]), window_block.dtype
            ),
        ],
        axis=1,
    )
    cross_sum = add_cross(empty_sum, widened, my_offsets, all_channels).astype(jnp.bfloat16)
    lagged = (
        jnp.einsum(
            "ocpk,pkl->ocl",
            lax.all_to_all(cross_sum, "gx", split_axis=1, concat_axis=3, tiled=True),
            inverse,
            preferred_element_type=jnp.float32,
        )
        * norm_scale
    )
    return lagged.astype(jnp.bfloat16)


def solution(mesh):
    return jax.shard_map(
        local,
        mesh=mesh,
        in_specs=(P("gx", "gy", None), P(), P()),
        out_specs=P("gy", "gx", None),
        check_vma=False,
    )
```

profile of v0, /device:TPU:0, one launch (start us, length us, event | category | flops | bytes accessed | tf_op | source)
XLA Modules:
  0.0 180.3 jit_solution(6627129745590901906)
XLA Ops:
  8.0 4.5 %fusion.2 = f32[1024,2048]{1,0:T(8,128)S(1)} fusion(bf16[1024,1024]{1,0:T(8,128)(2,1)S(1)} %bitcast.101, bf16[1024,1024]{1,0:T(8,128)(2,1)S(1)} %bitcast.103, bf16[1024,1024]{1,0:T(8,128)(2,1)S(1)} %bitcast.102), kind=kOutput, calls=%fused_computation.14 | convolution fusion | flops 4303355904 | bytes 14680064 | tf_op jit(solution)/shard_map/dot_general | solution.py:84
  15.2 6.6 %add.157 = f32[2,8,32,2,1024]{4,3,2,1,0:T(2,128)} reshape(f32[512,2048]{1,0:T(8,128)} %slice_add_fusion) | data formatting | bytes 8388608 | tf_op jit(solution)/shard_map/add | solution.py:86
  21.8 6.9 %slice_add_fusion.1 = (f32[1,8,32,1,1024]{4,3,2,1,0:T(1,128)S(1)}, f32[1,8,32,1,1024]{4,3,2,1,0:T(1,128)S(1)}, f32[1,8,32,1,1024]{4,3,2,1,0:T(1,128)S(1)}) fusion(f32[2,8,32,2,1024]{4,3,2,1,0:T(2,128)} %add.157), kind=kLoop, calls=%fused_computation.41 | loop fusion | flops 262144 | bytes 7340032 | tf_op jit(solution)/shard_map/add | solution.py:92
  32.7 7.3 %all-to-all-start = ((bf16[8,2,4096]{2,1,0:T(2,128)(2,1)}), bf16[8,2,4096]{2,1,0:T(2,128)(2,1)S(1)}, u32[]{:S(2)}, u32[]{:S(2)}) async-start(bf16[8,2,4096]{2,1,0:T(2,128)(2,1)} %reshape.414), calls=%async_computation | async-start | bytes 262144 | tf_op jit(solution)/shard_map/all_to_all | solution.py:107
  40.0 7.3 %all-to-all-done = bf16[8,2,4096]{2,1,0:T(2,128)(2,1)S(1)} async-done(((bf16[8,2,4096]{2,1,0:T(2,128)(2,1)}), bf16[8,2,4096]{2,1,0:T(2,128)(2,1)S(1)}, u32[]{:S(2)}, u32[]{:S(2)}) %all-to-all-start) | async-done | bytes 131104 | tf_op jit(solution)/shard_map/all_to_all | solution.py:107
  49.3 7.2 %all_gather.3 = bf16[8,128,2,128]{3,1,2,0:T(8,128)(2,1)S(1)} all-gather(bf16[2,128,2,128]{3,1,2,0:T(8,128)(2,1)S(1)} %bitcast.105), channel_id=1, replica_groups=mesh['gx'=8,'gy'=4] {'gy'}, dimensions={0}, use_global_device_ids=true | all-gather | bytes 655360 | tf_op jit(solution)/shard_map/all_gather | solution.py:110
  57.3 4.0 %broadcast_in_dim.8.clone = f32[32,128,2,128]{3,2,0,1:T(2,128)} broadcast(f32[]{:T(128)} %constant.108.clone.1), dimensions={} | broadcast | bytes 4194308 | tf_op jit(solution)/shard_map/broadcast_in_dim | solution.py:109
  61.3 51.1 %while.13 = (s32[]{:T(128)}, f32[32,128,2,128]{3,2,0,1:T(2,128)}, f32[8,128,2,128]{3,0,1,2:T(8,128)S(1)}, s32[32]{0:T(128)S(1)}, bf16[8,256,2,128]{3,0,2,1:T(8,1...) while((s32[]{:T(128)}, f32[32,128,2,128]{3,2,0,1:T(2,128)}, ...), condition=%wide.region_6.7_spmd, body=%wide.region_3.6_spmd.sunk | while | flops 10747950 | bytes 38797656 | solution.py:46
  61.4 3.1 %gather_fusion = bf16[8,8,128,2,128]{4,1,3,2,0:T(8,128)(2,1)} fusion(bf16[8,256,2,128]{3,0,2,1:T(8,128)(2,1)S(1)} %get-tuple-element.219, s32[8]{0:T(128)S(1)} %fusion.52), kind=kCustom, calls=%fused_computation.clone.1 | custom fusion | bytes 8388736 | tf_op jit(solution)/shard_map/while/body/eval_jaxpr/vmap()/gather | solution.py:29
  64.5 2.9 %convert_element_type.142 = f32[8,8,128,2,128]{4,1,3,2,0:T(8,128)S(1)} convert(bf16[8,8,128,2,128]{4,1,3,2,0:T(8,128)(2,1)} %gather_fusion) | non-fusion elementwise | flops 2097152 | bytes 12582912 | tf_op jit(solution)/shard_map/while/body/eval_jaxpr/vmap()/convert_element_type | solution.py:29
  67.5 3.1 %add_reduce_fusion.2 = (f32[8,128,128]{2,1,0:T(8,128)S(1)}, f32[8,128,128]{2,1,0:T(8,128)S(1)}) fusion(f32[8,8,128,2,128]{4,1,3,2,0:T(8,128)S(1)} %convert_element_type.142, f32[8,128,128]{2,0,1:T(8,128)S(1)} %get-tuple-element.193, f32[8,128,128]{2,0,1:T(8,128)S(1)} %get-tuple-element.194), kind=kLoop, calls=%fused_computation.4.clone.1 | loop fusion | flops 8126464 | bytes 10485760 | tf_op jit(solution)/shard_map/while/body/eval_jaxpr/vmap()/reduce_sum | solution.py:30
  74.2 3.1 %gather_fusion = bf16[8,8,128,2,128]{4,1,3,2,0:T(8,128)(2,1)} fusion(bf16[8,256,2,128]{3,0,2,1:T(8,128)(2,1)S(1)} %get-tuple-element.219, s32[8]{0:T(128)S(1)} %fusion.52), kind=kCustom, calls=%fused_computation.clone.1 | custom fusion | bytes 8388736 | tf_op jit(solution)/shard_map/while/body/eval_jaxpr/vmap()/gather | solution.py:29
  77.2 2.9 %convert_element_type.142 = f32[8,8,128,2,128]{4,1,3,2,0:T(8,128)S(1)} convert(bf16[8,8,128,2,128]{4,1,3,2,0:T(8,128)(2,1)} %gather_fusion) | non-fusion elementwise | flops 2097152 | bytes 12582912 | tf_op jit(solution)/shard_map/while/body/eval_jaxpr/vmap()/convert_element_type | solution.py:29
  80.2 3.1 %add_reduce_fusion.2 = (f32[8,128,128]{2,1,0:T(8,128)S(1)}, f32[8,128,128]{2,1,0:T(8,128)S(1)}) fusion(f32[8,8,128,2,128]{4,1,3,2,0:T(8,128)S(1)} %convert_element_type.142, f32[8,128,128]{2,0,1:T(8,128)S(1)} %get-tuple-element.193, f32[8,128,128]{2,0,1:T(8,128)S(1)} %get-tuple-element.194), kind=kLoop, calls=%fused_computation.4.clone.1 | loop fusion | flops 8126464 | bytes 10485760 | tf_op jit(solution)/shard_map/while/body/eval_jaxpr/vmap()/reduce_sum | solution.py:30
  86.9 3.1 %gather_fusion = bf16[8,8,128,2,128]{4,1,3,2,0:T(8,128)(2,1)} fusion(bf16[8,256,2,128]{3,0,2,1:T(8,128)(2,1)S(1)} %get-tuple-element.219, s32[8]{0:T(128)S(1)} %fusion.52), kind=kCustom, calls=%fused_computation.clone.1 | custom fusion | bytes 8388736 | tf_op jit(solution)/shard_map/while/body/eval_jaxpr/vmap()/gather | solution.py:29
  93.0 3.1 %add_reduce_fusion.2 = (f32[8,128,128]{2,1,0:T(8,128)S(1)}, f32[8,128,128]{2,1,0:T(8,128)S(1)}) fusion(f32[8,8,128,2,128]{4,1,3,2,0:T(8,128)S(1)} %convert_element_type.142, f32[8,128,128]{2,0,1:T(8,128)S(1)} %get-tuple-element.193, f32[8,128,128]{2,0,1:T(8,128)S(1)} %get-tuple-element.194), kind=kLoop, calls=%fused_computation.4.clone.1 | loop fusion | flops 8126464 | bytes 10485760 | tf_op jit(solution)/shard_map/while/body/eval_jaxpr/vmap()/reduce_sum | solution.py:30
  99.7 3.1 %gather_fusion = bf16[8,8,128,2,128]{4,1,3,2,0:T(8,128)(2,1)} fusion(bf16[8,256,2,128]{3,0,2,1:T(8,128)(2,1)S(1)} %get-tuple-element.219, s32[8]{0:T(128)S(1)} %fusion.52), kind=kCustom, calls=%fused_computation.clone.1 | custom fusion | bytes 8388736 | tf_op jit(solution)/shard_map/while/body/eval_jaxpr/vmap()/gather | solution.py:29
  105.8 3.1 %add_reduce_fusion.2 = (f32[8,128,128]{2,1,0:T(8,128)S(1)}, f32[8,128,128]{2,1,0:T(8,128)S(1)}) fusion(f32[8,8,128,2,128]{4,1,3,2,0:T(8,128)S(1)} %convert_element_type.142, f32[8,128,128]{2,0,1:T(8,128)S(1)} %get-tuple-element.193, f32[8,128,128]{2,0,1:T(8,128)S(1)} %get-tuple-element.194), kind=kLoop, calls=%fused_computation.4.clone.1 | loop fusion | flops 8126464 | bytes 10485760 | tf_op jit(solution)/shard_map/while/body/eval_jaxpr/vmap()/reduce_sum | solution.py:30
  112.4 5.5 %convert_element_type.99 = bf16[32,128,2,128]{3,2,0,1:T(2,128)(2,1)} convert(f32[32,128,2,128]{3,2,0,1:T(2,128)} %get-tuple-element.99) | non-fusion elementwise | flops 1048576 | bytes 6291456 | tf_op jit(solution)/shard_map/convert_element_type | solution.py:120
  117.9 3.9 %all-to-all-start.1 = ((bf16[32,128,2,128]{3,2,0,1:T(2,128)(2,1)}), bf16[32,128,2,128]{3,2,0,1:T(2,128)(2,1)S(1)}, u32[]{:S(2)}, u32[]{:S(2)}) async-start(bf16[32,128,2,128]{3,2,0,1:T(2,128)(2,1)} %convert_element_type.99), calls=%async_computation.1 | async-start | bytes 4194304 | tf_op jit(solution)/shard_map/all_to_all | solution.py:124
  121.8 9.8 %cosine_convert_fusion = (bf16[1,1024,512]{2,1,0:T(8,128)(2,1)S(1)}, bf16[1,1024,512]{2,1,0:T(8,128)(2,1)}) fusion(s32[512]{0:T(512)S(1)} %iota_add_fusion, s32[1024]{0:T(1024)S(1)} %copy-done), kind=kLoop, calls=%fused_computation.35 | loop fusion | flops 8912896 | bytes 2103296 | tf_op jit(solution)/shard_map/convert
  131.6 38.9 %all-to-all-done.1 = bf16[32,128,2,128]{3,2,0,1:T(2,128)(2,1)S(1)} async-done(((bf16[32,128,2,128]{3,2,0,1:T(2,128)(2,1)}), bf16[32,128,2,128]{3,2,0,1:T(2,128)(2,1)S(1)}, u32[]{:S(2)}, u32[]{:S(2)}) %all-to-all-start.1) | async-done | bytes 2097184 | tf_op jit(solution)/shard_map/all_to_all | solution.py:124
  170.5 3.8 %copy.79 = bf16[32,8,16,2,128]{4,1,2,3,0:T(8,128)(2,1)} copy(bf16[32,8,16,2,128]{4,3,0,2,1:T(2,128)(2,1)S(1)} %bitcast.96) | data formatting | bytes 4194304 | tf_op jit(solution)/shard_map/all_to_all | solution.py:124
  177.1 3.3 %fusion.14 = bf16[32,16,512]{2,1,0:T(8,128)(2,1)} fusion(bf16[32,16,2,1024]{3,1,2,0:T(8,128)(2,1)S(1)} %all_to_all.33, bf16[1,1024,512]{2,1,0:T(8,128)(2,1)} %get-tuple-element.151, bf16[1,1024,512]{2,1,0:T(8,128)(2,1)S(1)} %get-tuple-element.150), kind=kOutput, calls=%fused_computation.39 | convolution fusion | flops 1075314688 | bytes 4718592 | tf_op jit(solution)/shard_map/ocpk,pkl->ocl/dot_general | solution.py:122
  (50 shorter events, 40.8 us)
Async XLA Ops:
  28.7 11.2 %copy-start.1 = (s32[128]{0:T(128)S(1)}, s32[128]{0:T(128)}, u32[]{:S(2)}) copy-start(s32[128]{0:T(128)} %param.7) | copy-start | bytes 1540
  32.7 14.6 %all-to-all-start = ((bf16[8,2,4096]{2,1,0:T(2,128)(2,1)}), bf16[8,2,4096]{2,1,0:T(2,128)(2,1)S(1)}, u32[]{:S(2)}, u32[]{:S(2)}) async-start(bf16[8,2,4096]{2,1,0:T(2,128)(2,1)} %reshape.414), calls=%async_computation | async-start | bytes 262144 | tf_op jit(solution)/shard_map/all_to_all | solution.py:107
  112.4 9.4 %copy-start = (s32[1024]{0:T(1024)S(1)}, s32[1024]{0:T(1024)}, u32[]{:S(2)}) copy-start(s32[1024]{0:T(1024)} %param.6) | copy-start | bytes 12292
  117.9 52.6 %all-to-all-start.1 = ((bf16[32,128,2,128]{3,2,0,1:T(2,128)(2,1)}), bf16[32,128,2,128]{3,2,0,1:T(2,128)(2,1)S(1)}, u32[]{:S(2)}, u32[]{:S(2)}) async-start(bf16[32,128,2,128]{3,2,0,1:T(2,128)(2,1)} %convert_element_type.99), calls=%async_computation.1 | async-start | bytes 4194304 | tf_op jit(solution)/shard_map/all_to_all | solution.py:124
where the time goes:
time: 181 us; the launch traced here: 180 us
  other arithmetic  63.3 us (35%)
  waiting for transfers between devices  46.1 us (25%)
  local copies, waits for them, and re-layouts  43.5 us (24%)
  starting transfers between devices  11.1 us (6%)
  matrix products  8.83 us (5%)
  blocking collectives  7.18 us (4%)
    all_to_all x1, waiting for transfers between devices, local(): lax.all_to_all(cross_sum, 'gx', split_axis=1, concat_axis=3, tiled=True)  38.9 us
    reduce_sum x4, other arithmetic, one_offset(): jnp.sum(own_part[:, :, 0] * theirs[:, :, 0] + own_part[:, :, 1] * theirs[...  12.3 us
    gather x4, local copies, waits for them, and re-layouts, one_offset(): lax.dynamic_slice_in_dim(window_block, shift_by, own_count, 1)  12.2 us
    convert_element_type x4, other arithmetic, one_offset(): lax.dynamic_slice_in_dim(window_block, shift_by, own_count, 1)  11.7 us
    another operation x2, other arithmetic  11.3 us
    dynamic_update_slice x4, other arithmetic, one_group(): lax.dynamic_update_slice_in_dim(carried, current + update, group_index *...  8.78 us
    all_to_all x1, starting transfers between devices, local(): lax.all_to_all(white, 'gx', split_axis=3, concat_axis=1, tiled=True)  7.27 us
    all_to_all x1, waiting for transfers between devices, local(): lax.all_to_all(white, 'gx', split_axis=3, concat_axis=1, tiled=True)  7.26 us
  transfers between devices with their start and end apart: 2, of which 2 were waited for; matrix products, arithmetic and copies ran while one was open for 5% of the time, Pallas kernels for 0%

commit v1 on v0

--- a/solution.py
+++ b/solution.py
@@ -6,6 +6,17 @@
 
 SAMPLES = 8192
 LAGS = 512
+
+
+def turned_line(block, mesh_axis, d):
+    size = lax.axis_size(mesh_axis)
+    route = [(i, (i + 1) % size) for i in range(size)]
+    parts = [block]
+    for far in range(1, size):
+        parts = [lax.ppermute(parts[0], mesh_axis, route), *parts]
+    out = jnp.concatenate(parts, axis=d)
+    places = (lax.axis_index(mesh_axis) + 1) * parts[-1].shape[d]
+    return jnp.roll(out, places, axis=d)
 
 
 def inverse_table(kept_bins):
@@ -107,7 +118,7 @@
     freq_white = lax.all_to_all(white, "gx", split_axis=3, concat_axis=1, tiled=True)
     all_channels = freq_white.shape[1]
     empty_sum = jnp.zeros((off_dev, all_channels, 2, freq_white.shape[3]), jnp.float32)
-    window_block = lax.all_gather(freq_white, "gy", axis=0, tiled=True)
+    window_block = turned_line(freq_white, "gy", 0)
     widened = jnp.concatenate(
         [
             window_block,

time: 181 us -> 185 us (1.022)
  blocking collectives: 7.18 us -> 14.4 us
  starting transfers between devices: 11.1 us -> 3.92 us
  waiting for transfers between devices: 46.1 us -> 50.8 us
    all_to_all x0 -> x1, blocking collectives: none -> 14.4 us  [local(): lax.all_to_all(white, 'gx', split_axis=3, concat_axis=1, tiled=True)]
    ppermute x0 -> x3, waiting for transfers between devices: none -> 13.1 us  [turned_line(): parts = [lax.ppermute(parts[0], mesh_axis, route), *parts]]
    all_to_all x1 -> x0, starting transfers between devices: 7.27 us -> none  [local(): lax.all_to_all(white, 'gx', split_axis=3, concat_axis=1, tiled=True)]
    all_to_all x1 -> x0, waiting for transfers between devices: 7.26 us -> none  [local(): lax.all_to_all(white, 'gx', split_axis=3, concat_axis=1, tiled=True)]
    all_gather x1 -> x0, blocking collectives: 7.18 us -> none  [local(): window_block = lax.all_gather(freq_white, 'gy', axis=0, tiled=True)]
  transfers between devices with their start and end apart: 2 -> 4, of which waited for: 2 -> 4; matrix products, arithmetic and copies ran while one was open for 5% -> 5% of each run, Pallas kernels for 0% -> 0%
where the time goes in v1:
time: 185 us
  other arithmetic  63.3 us (34%)
  waiting for transfers between devices  50.8 us (27%)
  local copies, waits for them, and re-layouts  43 us (23%)
  blocking collectives  14.4 us (8%)
  matrix products  8.83 us (5%)
  starting transfers between devices  3.92 us (2%)
    all_to_all x1, waiting for transfers between devices, local(): lax.all_to_all(cross_sum, 'gx', split_axis=1, concat_axis=3, tiled=True)  37.7 us
    all_to_all x1, blocking collectives, local(): lax.all_to_all(white, 'gx', split_axis=3, concat_axis=1, tiled=True)  14.4 us
    ppermute x3, waiting for transfers between devices, turned_line(): parts = [lax.ppermute(parts[0], mesh_axis, route), *parts]  13.1 us
    reduce_sum x4, other arithmetic, one_offset(): jnp.sum(own_part[:, :, 0] * theirs[:, :, 0] + own_part[:, :, 1] * theirs[...  12.3 us
    gather x4, local copies, waits for them, and re-layouts, one_offset(): lax.dynamic_slice_in_dim(window_block, shift_by, own_count, 1)  12.2 us
    convert_element_type x4, other arithmetic, one_offset(): lax.dynamic_slice_in_dim(window_block, shift_by, own_count, 1)  11.7 us
    another operation x2, other arithmetic  11.3 us
    dynamic_update_slice x4, other arithmetic, one_group(): lax.dynamic_update_slice_in_dim(carried, current + update, group_index *...  8.8 us
  transfers between devices with their start and end apart: 4, of which 4 were waited for; matrix products, arithmetic and copies ran while one was open for 5% of the time, Pallas kernels for 0%

profile of v1, /device:TPU:0, one launch (start us, length us, event | category | flops | bytes accessed | tf_op | source)
XLA Modules:
  0.0 184.6 jit_solution(1332663557886934912)
XLA Ops:
  8.0 4.5 %fusion.2 = f32[1024,2048]{1,0:T(8,128)S(1)} fusion(bf16[1024,1024]{1,0:T(8,128)(2,1)S(1)} %bitcast.101, bf16[1024,1024]{1,0:T(8,128)(2,1)S(1)} %bitcast.103, bf16[1024,1024]{1,0:T(8,128)(2,1)S(1)} %bitcast.102), kind=kOutput, calls=%fused_computation.14 | convolution fusion | flops 4303355904 | bytes 14680064 | tf_op jit(solution)/shard_map/dot_general | solution.py:95
  15.3 6.6 %add.170 = f32[2,8,32,2,1024]{4,3,2,1,0:T(2,128)} reshape(f32[512,2048]{1,0:T(8,128)} %slice_add_fusion) | data formatting | bytes 8388608 | tf_op jit(solution)/shard_map/add | solution.py:97
  21.9 6.9 %slice_add_fusion.1 = (f32[1,8,32,1,1024]{4,3,2,1,0:T(1,128)S(1)}, f32[1,8,32,1,1024]{4,3,2,1,0:T(1,128)S(1)}, f32[1,8,32,1,1024]{4,3,2,1,0:T(1,128)S(1)}) fusion(f32[2,8,32,2,1024]{4,3,2,1,0:T(2,128)} %add.170), kind=kLoop, calls=%fused_computation.41 | loop fusion | flops 262144 | bytes 7340032 | tf_op jit(solution)/shard_map/add | solution.py:103
  32.0 14.4 %all_to_all.36 = bf16[8,2,4096]{2,1,0:T(2,128)(2,1)S(1)} all-to-all(bf16[8,2,4096]{2,1,0:T(2,128)(2,1)S(1)} %reshape.414), channel_id=1, replica_groups=mesh['gx'=8,'gy'=4] {'gx'}, dimensions={0} | all-to-all | bytes 262144 | tf_op jit(solution)/shard_map/all_to_all | solution.py:118
  48.5 4.4 %collective-permute-done = bf16[2,128,2,128]{3,1,2,0:T(8,128)(2,1)S(1)} collective-permute-done((bf16[2,128,2,128]{3,1,2,0:T(8,128)(2,1)S(1)}, bf16[2,128,2,128]{3,1,2,0:T(8,128)(2,1)S(1)}, u32[]{:S(2)}, u32[]{:S(2)}) %collective-permute-start) | collective-permute-done | bytes 131104 | tf_op jit(solution)/shard_map/ppermute | solution.py:16
  52.9 4.4 %collective-permute-done.1 = bf16[2,128,2,128]{3,1,2,0:T(8,128)(2,1)S(1)} collective-permute-done((bf16[2,128,2,128]{3,1,2,0:T(8,128)(2,1)S(1)}, bf16[2,128,2,128]{3,1,2,0:T(8,128)(2,1)S(1)}, u32[]{:S(2)}, u32[]{:S(2)}) %collective-permute-start.1) | collective-permute-done | bytes 131104 | tf_op jit(solution)/shard_map/ppermute | solution.py:16
  57.4 4.3 %collective-permute-done.2 = bf16[2,128,2,128]{3,1,2,0:T(8,128)(2,1)S(1)} collective-permute-done((bf16[2,128,2,128]{3,1,2,0:T(8,128)(2,1)S(1)}, bf16[2,128,2,128]{3,1,2,0:T(8,128)(2,1)S(1)}, u32[]{:S(2)}, u32[]{:S(2)}) %collective-permute-start.2) | collective-permute-done | bytes 131104 | tf_op jit(solution)/shard_map/ppermute | solution.py:16
  62.8 4.0 %broadcast_in_dim.8.clone = f32[32,128,2,128]{3,2,0,1:T(2,128)} broadcast(f32[]{:T(128)} %constant.125.clone.1), dimensions={} | broadcast | bytes 4194308 | tf_op jit(solution)/shard_map/broadcast_in_dim | solution.py:120
  66.8 51.1 %while.13 = (s32[]{:T(128)}, f32[32,128,2,128]{3,2,0,1:T(2,128)}, f32[8,128,2,128]{3,0,1,2:T(8,128)S(1)}, s32[32]{0:T(128)S(1)}, bf16[8,256,2,128]{3,0,2,1:T(8,1...) while((s32[]{:T(128)}, f32[32,128,2,128]{3,2,0,1:T(2,128)}, ...), condition=%wide.region_6.7_spmd, body=%wide.region_3.6_spmd.sunk | while | flops 10747950 | bytes 38797656 | solution.py:57
  66.9 3.1 %gather_fusion = bf16[8,8,128,2,128]{4,1,3,2,0:T(8,128)(2,1)} fusion(bf16[8,256,2,128]{3,0,2,1:T(8,128)(2,1)S(1)} %get-tuple-element.219, s32[8]{0:T(128)S(1)} %fusion.52), kind=kCustom, calls=%fused_computation.clone.1 | custom fusion | bytes 8388736 | tf_op jit(solution)/shard_map/while/body/eval_jaxpr/vmap()/gather | solution.py:40
  69.9 2.9 %convert_element_type.142 = f32[8,8,128,2,128]{4,1,3,2,0:T(8,128)S(1)} convert(bf16[8,8,128,2,128]{4,1,3,2,0:T(8,128)(2,1)} %gather_fusion) | non-fusion elementwise | flops 2097152 | bytes 12582912 | tf_op jit(solution)/shard_map/while/body/eval_jaxpr/vmap()/convert_element_type | solution.py:40
  73.0 3.1 %add_reduce_fusion.2 = (f32[8,128,128]{2,1,0:T(8,128)S(1)}, f32[8,128,128]{2,1,0:T(8,128)S(1)}) fusion(f32[8,8,128,2,128]{4,1,3,2,0:T(8,128)S(1)} %convert_element_type.142, f32[8,128,128]{2,0,1:T(8,128)S(1)} %get-tuple-element.193, f32[8,128,128]{2,0,1:T(8,128)S(1)} %get-tuple-element.194), kind=kLoop, calls=%fused_computation.4.clone.1 | loop fusion | flops 8126464 | bytes 10485760 | tf_op jit(solution)/shard_map/while/body/eval_jaxpr/vmap()/reduce_sum | solution.py:41
  79.7 3.1 %gather_fusion = bf16[8,8,128,2,128]{4,1,3,2,0:T(8,128)(2,1)} fusion(bf16[8,256,2,128]{3,0,2,1:T(8,128)(2,1)S(1)} %get-tuple-element.219, s32[8]{0:T(128)S(1)} %fusion.52), kind=kCustom, calls=%fused_computation.clone.1 | custom fusion | bytes 8388736 | tf_op jit(solution)/shard_map/while/body/eval_jaxpr/vmap()/gather | solution.py:40
  85.7 3.1 %add_reduce_fusion.2 = (f32[8,128,128]{2,1,0:T(8,128)S(1)}, f32[8,128,128]{2,1,0:T(8,128)S(1)}) fusion(f32[8,8,128,2,128]{4,1,3,2,0:T(8,128)S(1)} %convert_element_type.142, f32[8,128,128]{2,0,1:T(8,128)S(1)} %get-tuple-element.193, f32[8,128,128]{2,0,1:T(8,128)S(1)} %get-tuple-element.194), kind=kLoop, calls=%fused_computation.4.clone.1 | loop fusion | flops 8126464 | bytes 10485760 | tf_op jit(solution)/shard_map/while/body/eval_jaxpr/vmap()/reduce_sum | solution.py:41
  92.4 3.1 %gather_fusion = bf16[8,8,128,2,128]{4,1,3,2,0:T(8,128)(2,1)} fusion(bf16[8,256,2,128]{3,0,2,1:T(8,128)(2,1)S(1)} %get-tuple-element.219, s32[8]{0:T(128)S(1)} %fusion.52), kind=kCustom, calls=%fused_computation.clone.1 | custom fusion | bytes 8388736 | tf_op jit(solution)/shard_map/while/body/eval_jaxpr/vmap()/gather | solution.py:40
  98.5 3.1 %add_reduce_fusion.2 = (f32[8,128,128]{2,1,0:T(8,128)S(1)}, f32[8,128,128]{2,1,0:T(8,128)S(1)}) fusion(f32[8,8,128,2,128]{4,1,3,2,0:T(8,128)S(1)} %convert_element_type.142, f32[8,128,128]{2,0,1:T(8,128)S(1)} %get-tuple-element.193, f32[8,128,128]{2,0,1:T(8,128)S(1)} %get-tuple-element.194), kind=kLoop, calls=%fused_computation.4.clone.1 | loop fusion | flops 8126464 | bytes 10485760 | tf_op jit(solution)/shard_map/while/body/eval_jaxpr/vmap()/reduce_sum | solution.py:41
  105.2 3.1 %gather_fusion = bf16[8,8,128,2,128]{4,1,3,2,0:T(8,128)(2,1)} fusion(bf16[8,256,2,128]{3,0,2,1:T(8,128)(2,1)S(1)} %get-tuple-element.219, s32[8]{0:T(128)S(1)} %fusion.52), kind=kCustom, calls=%fused_computation.clone.1 | custom fusion | bytes 8388736 | tf_op jit(solution)/shard_map/while/body/eval_jaxpr/vmap()/gather | solution.py:40
  111.3 3.1 %add_reduce_fusion.2 = (f32[8,128,128]{2,1,0:T(8,128)S(1)}, f32[8,128,128]{2,1,0:T(8,128)S(1)}) fusion(f32[8,8,128,2,128]{4,1,3,2,0:T(8,128)S(1)} %convert_element_type.142, f32[8,128,128]{2,0,1:T(8,128)S(1)} %get-tuple-element.193, f32[8,128,128]{2,0,1:T(8,128)S(1)} %get-tuple-element.194), kind=kLoop, calls=%fused_computation.4.clone.1 | loop fusion | flops 8126464 | bytes 10485760 | tf_op jit(solution)/shard_map/while/body/eval_jaxpr/vmap()/reduce_sum | solution.py:41
  117.9 5.5 %convert_element_type.99 = bf16[32,128,2,128]{3,2,0,1:T(2,128)(2,1)} convert(f32[32,128,2,128]{3,2,0,1:T(2,128)} %get-tuple-element.99) | non-fusion elementwise | flops 1048576 | bytes 6291456 | tf_op jit(solution)/shard_map/convert_element_type | solution.py:131
  123.4 3.9 %all-to-all-start.1 = ((bf16[32,128,2,128]{3,2,0,1:T(2,128)(2,1)}), bf16[32,128,2,128]{3,2,0,1:T(2,128)(2,1)S(1)}, u32[]{:S(2)}, u32[]{:S(2)}) async-start(bf16[32,128,2,128]{3,2,0,1:T(2,128)(2,1)} %convert_element_type.99), calls=%async_computation.1 | async-start | bytes 4194304 | tf_op jit(solution)/shard_map/all_to_all | solution.py:135
  127.3 9.8 %cosine_convert_fusion = (bf16[1,1024,512]{2,1,0:T(8,128)(2,1)S(1)}, bf16[1,1024,512]{2,1,0:T(8,128)(2,1)}) fusion(s32[512]{0:T(512)S(1)} %iota_add_fusion, s32[1024]{0:T(1024)S(1)} %copy-done), kind=kLoop, calls=%fused_computation.35 | loop fusion | flops 8912896 | bytes 2103296 | tf_op jit(solution)/shard_map/convert
  137.1 37.7 %all-to-all-done.1 = bf16[32,128,2,128]{3,2,0,1:T(2,128)(2,1)S(1)} async-done(((bf16[32,128,2,128]{3,2,0,1:T(2,128)(2,1)}), bf16[32,128,2,128]{3,2,0,1:T(2,128)(2,1)S(1)}, u32[]{:S(2)}, u32[]{:S(2)}) %all-to-all-start.1) | async-done | bytes 2097184 | tf_op jit(solution)/shard_map/all_to_all | solution.py:135
  174.8 3.8 %copy.79 = bf16[32,8,16,2,128]{4,1,2,3,0:T(8,128)(2,1)} copy(bf16[32,8,16,2,128]{4,3,0,2,1:T(2,128)(2,1)S(1)} %bitcast.96) | data formatting | bytes 4194304 | tf_op jit(solution)/shard_map/all_to_all | solution.py:135
  181.3 3.3 %fusion.14 = bf16[32,16,512]{2,1,0:T(8,128)(2,1)} fusion(bf16[32,16,2,1024]{3,1,2,0:T(8,128)(2,1)S(1)} %all_to_all.33, bf16[1,1024,512]{2,1,0:T(8,128)(2,1)} %get-tuple-element.151, bf16[1,1024,512]{2,1,0:T(8,128)(2,1)S(1)} %get-tuple-element.150), kind=kOutput, calls=%fused_computation.39 | convolution fusion | flops 1075314688 | bytes 4718592 | tf_op jit(solution)/shard_map/ocpk,pkl->ocl/dot_general | solution.py:133
  (63 shorter events, 43.4 us)
Async XLA Ops:
  28.7 28.6 %copy-start.1 = (s32[128]{0:T(128)S(1)}, s32[128]{0:T(128)}, u32[]{:S(2)}) copy-start(s32[128]{0:T(128)} %param.7) | copy-start | bytes 1540
  48.4 4.4 %collective-permute-start = (bf16[2,128,2,128]{3,1,2,0:T(8,128)(2,1)S(1)}, bf16[2,128,2,128]{3,1,2,0:T(8,128)(2,1)S(1)}, u32[]{:S(2)}, u32[]{:S(2)}) collective-permute-start(bf16[2,128,2,128]{3,1,2,0:T(8,128)(2,1)S(1)} %bitcast.105), channel_id=1, source_target_pairs={{0,1},{1,2},{2,3},{3,0},{4,5},{5,6},{6,7},{7,4},{8,9},{9,10},{10,1... | collective-permute-start | bytes 393224 | tf_op jit(solution)/shard_map/ppermute | solution.py:16
  52.9 4.4 %collective-permute-start.1 = (bf16[2,128,2,128]{3,1,2,0:T(8,128)(2,1)S(1)}, bf16[2,128,2,128]{3,1,2,0:T(8,128)(2,1)S(1)}, u32[]{:S(2)}, u32[]{:S(2)}) collective-permute-start(bf16[2,128,2,128]{3,1,2,0:T(8,128)(2,1)S(1)} %collective-permute-done), channel_id=1, source_target_pairs={{0,1},{1,2},{2,3},{3,0},{4,5},{5,6},{6,7},{7,4},{8,9},{9,10},{10,1... | collective-permute-start | bytes 393224 | tf_op jit(solution)/shard_map/ppermute | solution.py:16
  57.3 4.4 %collective-permute-start.2 = (bf16[2,128,2,128]{3,1,2,0:T(8,128)(2,1)S(1)}, bf16[2,128,2,128]{3,1,2,0:T(8,128)(2,1)S(1)}, u32[]{:S(2)}, u32[]{:S(2)}) collective-permute-start(bf16[2,128,2,128]{3,1,2,0:T(8,128)(2,1)S(1)} %collective-permute-done.1), channel_id=1, source_target_pairs={{0,1},{1,2},{2,3},{3,0},{4,5},{5,6},{6,7},{7,4},{8,9},{9,10},{10,1... | collective-permute-start | bytes 393224 | tf_op jit(solution)/shard_map/ppermute | solution.py:16
  117.9 9.4 %copy-start = (s32[1024]{0:T(1024)S(1)}, s32[1024]{0:T(1024)}, u32[]{:S(2)}) copy-start(s32[1024]{0:T(1024)} %param.6) | copy-start | bytes 12292
  123.4 51.4 %all-to-all-start.1 = ((bf16[32,128,2,128]{3,2,0,1:T(2,128)(2,1)}), bf16[32,128,2,128]{3,2,0,1:T(2,128)(2,1)S(1)}, u32[]{:S(2)}, u32[]{:S(2)}) async-start(bf16[32,128,2,128]{3,2,0,1:T(2,128)(2,1)} %convert_element_type.99), calls=%async_computation.1 | async-start | bytes 4194304 | tf_op jit(solution)/shard_map/all_to_all | solution.py:135
